TPU v7x, 256 devices: a whole 4x4x8 slice. The times are simulated.
256 devices in a mesh: lon: 16 (over z, core), lat: 16 (over x, y).
Axes of the slice: x: 4, y: 4, z: 8, core: 2. Of those that a mesh axis runs over, the one named last changes fastest.
Arguments:
- state: float32 [16, 512, 4096], P(None, 'lat', 'lon'), may hold values from -6 to 6
- coef_lon: float32 [512, 4096], P('lat', 'lon'), may hold values from 0.2 to 0.24
- coef_lat: float32 [512, 4096], P('lat', 'lon'), may hold values from 0.2 to 0.24
- land_sea: int32 [512, 4096], P('lat', 'lon'), may hold values 0 or 1
- send_cols: int32 [16, 65536], P('lat', 'lon'), may hold values from 0 to 8191
- send_count: int32 [16, 256], P('lat', 'lon'), may hold values from 32 to 256, as said below
- obs_value: float32 [16, 16, 65536], P(None, 'lat', 'lon'), may hold values from -6 to 6
- obs_weight: float32 [16, 16, 65536], P(None, 'lat', 'lon'), may hold values from 0.25 to 4
Outputs:
- increment: float32 [16, 512, 4096], P(None, 'lat', 'lon')
Inputs may be any that keep to these rules, and one draw needn't show every extreme that they name: `send_count`: at most 256 live slots go from one device to one peer; in every latitude band some receiving device gets 256 from every device of the band, which one drawn from the seed. `send_cols`: entries index a column of the sending device's own block, row-major over its 32 x 256 cells.
All inputs are finite; a program needn't handle non-finite values. No bound on the sum of `land_sea` on one device may be relied on, other than what follows from the above.
Results may differ from a plain program's by a relative error of at most 0.00002.
Values sent between devices are 32-bit elements; how exact they have to be, the bound alone decides.
No kernel may reach another device: no remote copies, remote signals or barrier semaphores. Data moves between devices by JAX's collectives and lax.ppermute only.
A program may use at most 64 MiB of HBM per device.

v0:
```python
import jax
import jax.numpy as jnp
from jax import lax
from jax.sharding import PartitionSpec as P

PASSES = 8


def with_halo(block, sides, width):
    for axis, dim in sides:
        count = lax.axis_size(axis)
        forward = [(i, i + 1) for i in range(count - 1)]
        forward.append((count - 1, 0))
        backward = [(target, source) for source, target in forward]
        low = lax.ppermute(
            lax.slice_in_dim(block, block.shape[dim] - width, None, axis=dim), axis, forward
        )
        high = lax.ppermute(lax.slice_in_dim(block, 0, width, axis=dim), axis, backward)
        block = jnp.concatenate([low, block, high], axis=dim)
    return block


def one_pass(layer_field, east_face, north_face):
    flux_east = east_face * (layer_field[:, :, 1:] - layer_field[:, :, :-1])
    flux_north = north_face * (layer_field[:, 1:, :] - layer_field[:, :-1, :])
    return (
        layer_field[:, 1:-1, 1:-1]
        + flux_east[:, 1:-1, 1:]
        - flux_east[:, 1:-1, :-1]
        + flux_north[:, 1:, 1:-1]
        - flux_north[:, :-1, 1:-1]
    )


def body(state, coef_lon, coef_lat, land_sea, send_cols, send_count, obs_value, obs_weight):
    levels, rows_here, cols_here = state.shape
    lon_count = lax.axis_size("lon")
    lat_count = lax.axis_size("lat")
    slots = send_cols.shape[1]
    capacity = slots // lon_count
    columns = state.reshape(levels, rows_here * cols_here)
    targets = send_cols[0]
    slot_index = jnp.arange(slots, dtype=jnp.int32)
    limits = jnp.broadcast_to(send_count[0][:, None], (lon_count, capacity)).reshape(slots)
    usable = jnp.where(slot_index % capacity < limits, 1.0, 0.0).astype(jnp.float32)
    held = jnp.stack([obs_value[:, 0, :], obs_weight[:, 0, :]])
    at_owner = lax.all_to_all(held, "lon", split_axis=2, concat_axis=2, tiled=True)
    at_column = jnp.take(columns, targets, axis=1)
    weighted = at_owner[1] * (at_owner[0] - at_column) * usable
    sea = land_sea.astype(jnp.float32)
    gradient = jnp.zeros((levels, rows_here * cols_here), jnp.float32).at[:, targets].add(weighted)
    gradient = gradient.reshape(levels, rows_here, cols_here) * sea[None]
    rim_width = PASSES
    stacked = jnp.stack([sea, coef_lon, coef_lat])
    padded = with_halo(stacked, (("lon", 2), ("lat", 1)), rim_width)
    lat_index = lax.axis_index("lat")
    row_place = jnp.arange(rows_here + 2 * rim_width, dtype=jnp.int32)
    outside = (row_place < rim_width) & (lat_index == 0) | (row_place >= rows_here + rim_width) & (
        lat_index == lat_count - 1
    )
    inside = jnp.where(outside, 0.0, 1.0).astype(jnp.float32)[:, None]
    sea_rim = padded[0] * inside
    east_face = padded[1][:, :-1] * sea_rim[:, :-1] * sea_rim[:, 1:]
    north_face = padded[2][:-1, :] * sea_rim[:-1, :] * sea_rim[1:, :]
    field = with_halo(gradient, (("lon", 2), ("lat", 1)), rim_width)
    for step_number in range(PASSES):
        high, wide = (field.shape[1], field.shape[2])
        field = one_pass(
            field,
            east_face[step_number : step_number + high, step_number : step_number + wide - 1],
            north_face[step_number : step_number + high - 1, step_number : step_number + wide],
        )
    gradient = field
    return gradient


def solution(mesh):
    placed = (
        P(None, "lat", "lon"),
        P("lat", "lon"),
        P("lat", "lon"),
        P("lat", "lon"),
        P("lat", "lon"),
        P("lat", "lon"),
        P(None, "lat", "lon"),
        P(None, "lat", "lon"),
    )
    return jax.shard_map(
        body, mesh=mesh, in_specs=placed, out_specs=P(None, "lat", "lon"), check_vma=False
    )
```

profile of v0, /device:TPU:32, one launch (start us, length us, event | category | flops | bytes accessed | tf_op | source)
XLA Modules:
  0.0 152.6 jit_solution(4161188813281966988)
XLA Ops:
  0.0 1.3 copy_bitcast_fusion
  1.4 4.4 %copy.17 = f32[2,16,4096]{1,0,2:T(2,128)} copy(f32[2,16,4096]{2,1,0:T(8,128)S(1)} %pad_maximum_fusion.1) | data formatting | bytes 1048576 | tf_op jit(solution)/shard_map/stack | solution.py:46
  5.8 8.0 %reshape.116 = f32[16,1,8192]{2,1,0:T(1,128)} reshape(f32[4096,2,16]{2,1,0:T(2,128)} %bitcast.49) | data formatting | bytes 1048576
  13.7 8.7 %all-to-all-start = ((f32[16,1,8192]{2,1,0:T(1,128)}), f32[16,1,8192]{2,1,0:T(1,128)S(1)}, u32[]{:S(2)}, u32[]{:S(2)}) async-start(f32[16,1,8192]{2,1,0:T(1,128)} %reshape.116), calls=%async_computation | async-start | bytes 1048576 | tf_op jit(solution)/shard_map/all_to_all | solution.py:47
  22.6 0.1 collective-permute-start.5
  22.7 0.4 collective-permute-start.4
  23.3 11.7 %collective-permute-done.5 = f32[3,32,8]{2,1,0:T(8,128)S(1)} collective-permute-done((f32[3,32,8]{2,1,0:T(8,128)S(1)}, f32[3,32,8]{2,1,0:T(8,128)S(1)}, u32[]{:S(2)}, u32[]{:S(2)}) %collective-permute-start.5) | collective-permute-done | bytes 3104 | tf_op jit(solution)/shard_map/ppermute | solution.py:18
  35.0 0.1 pad_maximum_fusion.11
  35.1 5.3 %collective-permute-start.7 = (f32[3,8,272]{2,1,0:T(8,128)S(1)}, f32[3,8,272]{2,1,0:T(8,128)S(1)}, u32[]{:S(2)}, u32[]{:S(2)}) collective-permute-start(f32[3,8,272]{2,1,0:T(8,128)S(1)} %get-tuple-element.12), channel_id=1, source_target_pairs={{1,0},{2,1},{3,2},{4,3},{5,4},{6,5},{7,6},{8,7},{9,8},{10,9},{11,1... | collective-permute-start | bytes 78344 | tf_op jit(solution)/shard_map/ppermute | solution.py:18
  40.4 2.6 %copy.20 = f32[16,32,256]{0,2,1:T(8,128)} copy(f32[16,32,256]{2,1,0:T(8,128)S(1)} %copy-done.1) | data formatting | bytes 1048576 | tf_op args[0]
  43.1 4.6 %collective-permute-done.6 = f32[3,8,272]{2,1,0:T(8,128)S(1)} collective-permute-done((f32[3,8,272]{2,1,0:T(8,128)S(1)}, f32[3,8,272]{2,1,0:T(8,128)S(1)}, u32[]{:S(2)}, u32[]{:S(2)}) %collective-permute-start.6) | collective-permute-done | bytes 26144 | tf_op jit(solution)/shard_map/ppermute | solution.py:15
  47.7 0.1 pad_maximum_fusion.2
  47.9 0.5 broadcast.109
  48.4 1.9 %reduce = f32[16,8192]{1,0:T(8,128)S(1)} reduce(f32[16,1,8192]{2,1,0:T(1,128)S(1)} %all-to-all-done, f32[]{:T(128)} %broadcast.109), dimensions={1}, to_apply=%all_to_all.3.reduce_sub_computation | reduce | bytes 1048580 | tf_op jit(solution)/shard_map/all_to_all | solution.py:47
  50.3 7.0 %reshape.117 = f32[4096,2,16]{2,1,0:T(2,128)} reshape(f32[16,8192]{1,0:T(8,128)S(1)} %reduce) | data formatting | bytes 1048576
  57.3 7.6 %fusion.33 = (f32[1,16,4096]{1,0,2:T(1,128)S(1)}, f32[1,16,4096]{1,0,2:T(1,128)}) fusion(f32[2,16,4096]{1,0,2:T(2,128)} %bitcast.52), kind=kLoop, calls=%fused_computation.114 | loop fusion | bytes 1048576 | tf_op jit(solution)/shard_map/slice | solution.py:49
  64.9 51.2 %scatter_custom_fusion = f32[16,8192]{0,1:T(8,128)} fusion(s32[4096]{0:T(1024)S(1)} %bitcast.63, f32[16,4096]{0,1:T(8,128)} %bitcast.54, f32[16,4096]{0,1:T(8,128)S(1)} %bitcast.53, f32[]{:T(128)} %constant.19.clone.1, f32[]{:T(128)} %constant.23.clone.1, f32[4096]{0:T(1024)S(1)} %fusion.31, pred[4096]{0:T(1024)(128)(4,1)S(1)} %compare_and_fusion, ...), kind=kCustom, calls=%fused_computation.2 | custom fusion | flops 327680 | bytes 3444744 | tf_op jit(solution)/shard_map/scatter-add | solution.py:51
  116.1 2.9 %copy.21 = f32[16,32,256]{2,1,0:T(8,128)S(1)} copy(f32[16,32,256]{0,2,1:T(8,128)} %bitcast.51) | data formatting | bytes 1048576 | tf_op jit(solution)/shard_map/reshape | solution.py:52
  119.1 0.1 fusion.34
  119.2 0.8 collective-permute-start.1
  120.0 0.1 slice.453
  120.1 0.1 slice.464
  120.2 3.7 %collective-permute-done.1 = f32[16,32,8]{2,1,0:T(8,128)S(1)} collective-permute-done((f32[16,32,8]{2,1,0:T(8,128)S(1)}, f32[16,32,8]{2,1,0:T(8,128)S(1)}, u32[]{:S(2)}, u32[]{:S(2)}) %collective-permute-start.1) | collective-permute-done | bytes 16416 | tf_op jit(solution)/shard_map/ppermute | solution.py:18
  123.9 2.6 %collective-permute-done = f32[16,32,8]{2,1,0:T(8,128)S(1)} collective-permute-done((f32[16,32,8]{2,1,0:T(8,128)S(1)}, f32[16,32,8]{2,1,0:T(8,128)S(1)}, u32[]{:S(2)}, u32[]{:S(2)}) %collective-permute-start) | collective-permute-done | bytes 16416 | tf_op jit(solution)/shard_map/ppermute | solution.py:15
  126.5 0.2 pad_maximum_fusion.5
  126.7 0.9 collective-permute-start.3
  127.6 1.2 collective-permute-start.2
  128.8 0.1 slice_multiply_fusion.2
  128.9 0.1 slice.448
  129.0 0.1 slice.459
  129.0 0.1 slice.475
  129.1 0.1 slice.470
  129.2 0.1 slice.486
  129.3 0.1 slice.481
  129.4 0.1 slice.497
  129.5 0.1 slice.492
  129.6 0.1 slice.508
  129.9 3.0 %collective-permute-done.3 = f32[16,8,272]{2,1,0:T(8,128)S(1)} collective-permute-done((f32[16,8,272]{2,1,0:T(8,128)S(1)}, f32[16,8,272]{2,1,0:T(8,128)S(1)}, u32[]{:S(2)}, u32[]{:S(2)}) %collective-permute-start.3) | collective-permute-done | bytes 139296 | tf_op jit(solution)/shard_map/ppermute | solution.py:18
  132.9 4.6 %collective-permute-done.2 = f32[16,8,272]{2,1,0:T(8,128)S(1)} collective-permute-done((f32[16,8,272]{2,1,0:T(8,128)S(1)}, f32[16,8,272]{2,1,0:T(8,128)S(1)}, u32[]{:S(2)}, u32[]{:S(2)}) %collective-permute-start.2) | collective-permute-done | bytes 139296 | tf_op jit(solution)/shard_map/ppermute | solution.py:15
  137.5 0.3 pad_maximum_fusion
  137.9 0.2 fusion.13
  138.0 0.4 fusion.14
  138.4 1.4 slice_subtract_fusion.10
  139.9 0.2 fusion.11
  140.0 0.4 fusion.12
  140.4 1.4 slice_subtract_fusion.6
  141.9 0.2 fusion.9
  142.0 0.4 fusion.10
  142.4 1.4 slice_subtract_fusion.2
  143.9 0.2 fusion.7
  144.0 0.4 fusion.8
  144.4 1.2 slice_subtract_fusion.28
  145.6 0.1 fusion.24
  145.7 0.3 fusion.25
  146.1 1.2 slice_subtract_fusion.24
  147.3 0.1 fusion.22
  147.4 0.3 fusion.23
  147.8 1.2 slice_subtract_fusion.20
  149.0 0.1 fusion.20
  149.1 0.3 fusion.21
  149.4 1.2 slice_subtract_fusion.16
  150.6 0.1 fusion.18
  150.8 0.3 fusion.19
  151.1 1.5 slice_subtract_fusion.30
  (35 shorter events, 0.7 us)
Async XLA Ops:
  0.0 23.1 %copy-start = (s32[1,16]{1,0:T(1,128)S(1)}, s32[1,16]{1,0:T(1,128)}, u32[]{:S(2)}) copy-start(s32[1,16]{1,0:T(1,128)} %param.13) | copy-start | bytes 196
  5.8 16.7 %copy-start.5 = (s32[32,256]{1,0:T(8,128)S(1)}, s32[32,256]{1,0:T(8,128)}, u32[]{:S(2)}) copy-start(s32[32,256]{1,0:T(8,128)} %param.11) | copy-start | bytes 98308
  5.8 16.7 %copy-start.2 = (f32[32,256]{1,0:T(8,128)S(1)}, f32[32,256]{1,0:T(8,128)}, u32[]{:S(2)}) copy-start(f32[32,256]{1,0:T(8,128)} %param.10) | copy-start | bytes 98308
  5.8 16.7 %copy-start.3 = (f32[32,256]{1,0:T(8,128)S(1)}, f32[32,256]{1,0:T(8,128)}, u32[]{:S(2)}) copy-start(f32[32,256]{1,0:T(8,128)} %param.9) | copy-start | bytes 98308
  13.7 9.4 %copy-start.4 = (s32[1,4096]{1,0:T(1,128)S(1)}, s32[1,4096]{1,0:T(1,128)}, u32[]{:S(2)}) copy-start(s32[1,4096]{1,0:T(1,128)} %param.12) | copy-start | bytes 49156
  13.7 26.7 %copy-start.1 = (f32[16,32,256]{2,1,0:T(8,128)S(1)}, f32[16,32,256]{2,1,0:T(8,128)}, u32[]{:S(2)}) copy-start(f32[16,32,256]{2,1,0:T(8,128)} %param.8) | copy-start | bytes 1572868
  13.7 34.2 %all-to-all-start = ((f32[16,1,8192]{2,1,0:T(1,128)}), f32[16,1,8192]{2,1,0:T(1,128)S(1)}, u32[]{:S(2)}, u32[]{:S(2)}) async-start(f32[16,1,8192]{2,1,0:T(1,128)} %reshape.116), calls=%async_computation | async-start | bytes 1048576 | tf_op jit(solution)/shard_map/all_to_all | solution.py:47
  22.6 12.4 %collective-permute-start.5 = (f32[3,32,8]{2,1,0:T(8,128)S(1)}, f32[3,32,8]{2,1,0:T(8,128)S(1)}, u32[]{:S(2)}, u32[]{:S(2)}) collective-permute-start(f32[3,32,8]{2,1,0:T(8,128)S(1)} %get-tuple-element.14), channel_id=1, source_target_pairs={{16,0},{32,16},{48,32},{64,48},{80,64},{96,80},{112,96},{128,112},... | collective-permute-start | bytes 9224 | tf_op jit(solution)/shard_map/ppermute | solution.py:18
  22.7 12.3 %collective-permute-start.4 = (f32[3,32,8]{2,1,0:T(8,128)S(1)}, f32[3,32,8]{2,1,0:T(8,128)S(1)}, u32[]{:S(2)}, u32[]{:S(2)}) collective-permute-start(f32[3,32,8]{2,1,0:T(8,128)S(1)} %get-tuple-element.13), channel_id=1, source_target_pairs={{0,16},{16,32},{32,48},{48,64},{64,80},{80,96},{96,112},{112,128},... | collective-permute-start | bytes 9224 | tf_op jit(solution)/shard_map/ppermute | solution.py:15
  35.1 8.0 %collective-permute-start.7 = (f32[3,8,272]{2,1,0:T(8,128)S(1)}, f32[3,8,272]{2,1,0:T(8,128)S(1)}, u32[]{:S(2)}, u32[]{:S(2)}) collective-permute-start(f32[3,8,272]{2,1,0:T(8,128)S(1)} %get-tuple-element.12), channel_id=1, source_target_pairs={{1,0},{2,1},{3,2},{4,3},{5,4},{6,5},{7,6},{8,7},{9,8},{10,9},{11,1... | collective-permute-start | bytes 78344 | tf_op jit(solution)/shard_map/ppermute | solution.py:18
  40.4 7.3 %collective-permute-start.6 = (f32[3,8,272]{2,1,0:T(8,128)S(1)}, f32[3,8,272]{2,1,0:T(8,128)S(1)}, u32[]{:S(2)}, u32[]{:S(2)}) collective-permute-start(f32[3,8,272]{2,1,0:T(8,128)S(1)} %get-tuple-element.11), channel_id=1, source_target_pairs={{0,1},{1,2},{2,3},{3,4},{4,5},{5,6},{6,7},{7,8},{8,9},{9,10},{10,1... | collective-permute-start | bytes 78344 | tf_op jit(solution)/shard_map/ppermute | solution.py:15
  119.2 4.7 %collective-permute-start.1 = (f32[16,32,8]{2,1,0:T(8,128)S(1)}, f32[16,32,8]{2,1,0:T(8,128)S(1)}, u32[]{:S(2)}, u32[]{:S(2)}) collective-permute-start(f32[16,32,8]{2,1,0:T(8,128)S(1)} %get-tuple-element.10), channel_id=1, source_target_pairs={{16,0},{32,16},{48,32},{64,48},{80,64},{96,80},{112,96},{128,112},... | collective-permute-start | bytes 49160 | tf_op jit(solution)/shard_map/ppermute | solution.py:18
  120.0 6.5 %collective-permute-start = (f32[16,32,8]{2,1,0:T(8,128)S(1)}, f32[16,32,8]{2,1,0:T(8,128)S(1)}, u32[]{:S(2)}, u32[]{:S(2)}) collective-permute-start(f32[16,32,8]{2,1,0:T(8,128)S(1)} %get-tuple-element.9), channel_id=1, source_target_pairs={{0,16},{16,32},{32,48},{48,64},{64,80},{80,96},{96,112},{112,128},... | collective-permute-start | bytes 49160 | tf_op jit(solution)/shard_map/ppermute | solution.py:15
  126.7 6.2 %collective-permute-start.3 = (f32[16,8,272]{2,1,0:T(8,128)S(1)}, f32[16,8,272]{2,1,0:T(8,128)S(1)}, u32[]{:S(2)}, u32[]{:S(2)}) collective-permute-start(f32[16,8,272]{2,1,0:T(8,128)S(1)} %get-tuple-element.8), channel_id=1, source_target_pairs={{1,0},{2,1},{3,2},{4,3},{5,4},{6,5},{7,6},{8,7},{9,8},{10,9},{11,1... | collective-permute-start | bytes 417800 | tf_op jit(solution)/shard_map/ppermute | solution.py:18
  127.6 10.0 %collective-permute-start.2 = (f32[16,8,272]{2,1,0:T(8,128)S(1)}, f32[16,8,272]{2,1,0:T(8,128)S(1)}, u32[]{:S(2)}, u32[]{:S(2)}) collective-permute-start(f32[16,8,272]{2,1,0:T(8,128)S(1)} %get-tuple-element.7), channel_id=1, source_target_pairs={{0,1},{1,2},{2,3},{3,4},{4,5},{5,6},{6,7},{7,8},{8,9},{9,10},{10,1... | collective-permute-start | bytes 417800 | tf_op jit(solution)/shard_map/ppermute | solution.py:15
where the time goes:
time: 153 us
  other arithmetic  68.8 us (45%)
  local copies, waits for them, and re-layouts  35.8 us (23%)
  waiting for transfers between devices  30.2 us (20%)
  starting transfers between devices  17.4 us (11%)
    scatter-add x1, other arithmetic, body(): jnp.zeros((levels, rows_here * cols_here), jnp.float32).at[:, targets]  51.2 us
    unnamed x18, local copies, waits for them, and re-layouts  19 us
    ppermute x4, waiting for transfers between devices, with_halo(): lax.ppermute(lax.slice_in_dim(block, 0, width, axis=dim), axis, backward)  18.4 us
    ppermute x4, waiting for transfers between devices, with_halo(): lax.ppermute(lax.slice_in_dim(block, block.shape[dim] - width, None, axis...  11.8 us
    sub x8, other arithmetic, one_pass(): layer_field[:, 1:-1, 1:-1] + flux_east[:, 1:-1, 1:]  10.6 us
    all_to_all x1, starting transfers between devices, body(): lax.all_to_all(held, 'lon', split_axis=2, concat_axis=2, tiled=True)  8.72 us
    slice x1, local copies, waits for them, and re-layouts, body(): weighted = at_owner[1] * (at_owner[0] - at_column) * usable  7.62 us
    ppermute x4, starting transfers between devices, with_halo(): lax.ppermute(lax.slice_in_dim(block, 0, width, axis=dim), axis, backward)  7.1 us
  transfers between devices with their start and end apart: 9, of which 6 were waited for; matrix products, arithmetic and copies ran while one was open for 3% of the time, Pallas kernels for 0%

commit v1 on v0

--- a/solution.py
+++ b/solution.py
@@ -4,6 +4,29 @@
 from jax.sharding import PartitionSpec as P
 
 PASSES = 8
+
+
+def split_up(shard, dim, devices):
+    lengths = shard.shape
+    blocks = shard.reshape(*lengths[:dim], devices, lengths[dim] // devices, *lengths[dim + 1 :])
+    return jnp.moveaxis(blocks, dim, 0)
+
+
+def in_order(tiles, dim):
+    tiles = jnp.moveaxis(tiles, 0, dim)
+    dims = tiles.shape
+    return tiles.reshape(*dims[:dim], dims[dim] * dims[dim + 1], *dims[dim + 2 :])
+
+
+def exchange_in_pairs(x, axis, split_dim, concat_dim):
+    size, index = (lax.axis_size(axis), lax.axis_index(axis))
+    blocks = split_up(x, split_dim, size)
+    done = [blocks[index]]
+    for step in range(1, size):
+        sent = blocks[index ^ step]
+        done.append(lax.ppermute(sent, axis, [(i, i ^ step) for i in range(size)]))
+    blocks = jnp.stack(done)[index ^ jnp.arange(size)]
+    return in_order(blocks, concat_dim)
 
 
 def with_halo(block, sides, width):
@@ -44,7 +67,7 @@
     limits = jnp.broadcast_to(send_count[0][:, None], (lon_count, capacity)).reshape(slots)
     usable = jnp.where(slot_index % capacity < limits, 1.0, 0.0).astype(jnp.float32)
     held = jnp.stack([obs_value[:, 0, :], obs_weight[:, 0, :]])
-    at_owner = lax.all_to_all(held, "lon", split_axis=2, concat_axis=2, tiled=True)
+    at_owner = exchange_in_pairs(held, "lon", 2, 2)
     at_column = jnp.take(columns, targets, axis=1)
     weighted = at_owner[1] * (at_owner[0] - at_column) * usable
     sea = land_sea.astype(jnp.float32)

time: 153 us -> 131 us (0.86)
  the two profiles are of different devices: /device:TPU:32 before, /device:TPU:1 now
where the time goes in v1:
time: 131 us
  starting transfers between devices  46.2 us (35%)
  other arithmetic  44 us (34%)
  local copies, waits for them, and re-layouts  26 us (20%)
  waiting for transfers between devices  13.9 us (11%)
    ppermute x15, starting transfers between devices, exchange_in_pairs(): done.append(lax.ppermute(sent, axis, [(i, i ^ step) for i in range(size)]))  32.4 us
    scatter-add x1, other arithmetic, body(): jnp.zeros((levels, rows_here * cols_here), jnp.float32).at[:, targets]  24.7 us
    gather x2, local copies, waits for them, and re-layouts, body(): at_column = jnp.take(columns, targets, axis=1)  13.5 us
    sub x8, other arithmetic, one_pass(): layer_field[:, 1:-1, 1:-1] + flux_east[:, 1:-1, 1:]  10.6 us
    ppermute x4, starting transfers between devices, with_halo(): lax.ppermute(lax.slice_in_dim(block, 0, width, axis=dim), axis, backward)  8.96 us
    ppermute x4, waiting for transfers between devices, with_halo(): lax.ppermute(lax.slice_in_dim(block, block.shape[dim] - width, None, axis...  7.07 us
    unnamed x49, local copies, waits for them, and re-layouts  6.08 us
    ppermute x4, starting transfers between devices, with_halo(): lax.ppermute(lax.slice_in_dim(block, block.shape[dim] - width, None, axis...  4.91 us
  transfers between devices with their start and end apart: 23, of which 8 were waited for; matrix products, arithmetic and copies ran while one was open for 17% of the time, Pallas kernels for 0%

profile of v1, /device:TPU:1, one launch (start us, length us, event | category | flops | bytes accessed | tf_op | source)
XLA Modules:
  0.0 130.8 jit_solution(12651162301048609951)
XLA Ops:
  0.0 1.6 %reduce = f32[16,4096]{1,0:T(8,128)S(1)} reduce(f32[16,1,4096]{2,1,0:T(1,128)} %param.14, f32[]{:T(128)} %constant.87), dimensions={1}, to_apply=%param.14.reduce_sub_computation | reduce | bytes 524292 | tf_op args[6]
  1.9 0.6 reduce.1
  2.8 0.2 copy_dynamic-update-slice_fusion
  2.9 0.8 dynamic-slice_bitcast_fusion
  3.8 3.3 %collective-permute-start = (f32[2,16,256]{2,1,0:T(8,128)}, f32[2,16,256]{2,1,0:T(8,128)}, u32[]{:S(2)}, u32[]{:S(2)}) collective-permute-start(f32[2,16,256]{2,1,0:T(8,128)} %get-tuple-element.25), channel_id=1, source_target_pairs={{0,16},{16,0},{32,48},{48,32},{64,80},{80,64},{96,112},{112,96},{1... | collective-permute-start | bytes 98312 | tf_op jit(solution)/shard_map/ppermute | solution.py:27
  7.1 1.7 %collective-permute-start.2 = (f32[2,16,256]{2,1,0:T(8,128)}, f32[2,16,256]{2,1,0:T(8,128)}, u32[]{:S(2)}, u32[]{:S(2)}) collective-permute-start(f32[2,16,256]{2,1,0:T(8,128)} %get-tuple-element.23), channel_id=1, source_target_pairs={{0,48},{16,32},{32,16},{48,0},{64,112},{80,96},{96,80},{112,64},{1... | collective-permute-start | bytes 98312 | tf_op jit(solution)/shard_map/ppermute | solution.py:27
  9.0 0.5 collective-permute-start.20
  9.6 0.6 fusion.26
  10.2 0.5 collective-permute-done.19
  10.7 1.8 %collective-permute-done.20 = f32[3,32,8]{2,1,0:T(8,128)S(1)} collective-permute-done((f32[3,32,8]{2,1,0:T(8,128)S(1)}, f32[3,32,8]{2,1,0:T(8,128)S(1)}, u32[]{:S(2)}, u32[]{:S(2)}) %collective-permute-start.20) | collective-permute-done | bytes 3104 | tf_op jit(solution)/shard_map/ppermute | solution.py:41
  12.6 1.3 collective-permute-start.21
  13.8 3.7 %collective-permute-start.22 = (f32[3,8,272]{2,1,0:T(8,128)S(1)}, f32[3,8,272]{2,1,0:T(8,128)}, u32[]{:S(2)}, u32[]{:S(2)}) collective-permute-start(f32[3,8,272]{2,1,0:T(8,128)S(1)} %get-tuple-element.27), channel_id=1, source_target_pairs={{1,0},{2,1},{3,2},{4,3},{5,4},{6,5},{7,6},{8,7},{9,8},{10,9},{11,1... | collective-permute-start | bytes 78344 | tf_op jit(solution)/shard_map/ppermute | solution.py:41
  17.6 2.6 %copy.27 = f32[16,32,256]{0,2,1:T(8,128)} copy(f32[16,32,256]{2,1,0:T(8,128)S(1)} %copy-done.1) | data formatting | bytes 1048576 | tf_op args[0]
  20.2 13.0 %gather_fusion.1 = f32[4096,16]{1,0:T(8,128)S(1)} fusion(f32[16,8192]{0,1:T(8,128)} %bitcast.115, s32[4096]{0:T(1024)S(1)} %broadcast_clamp_fusion), kind=kCustom, calls=%fused_computation.1 | custom fusion | bytes 540672 | tf_op jit(solution)/shard_map/jit(_take)/gather | solution.py:71
  33.2 0.6 copy.28
  33.8 3.1 %collective-permute-start.3 = (f32[2,16,256]{2,1,0:T(8,128)}, f32[2,16,256]{2,1,0:T(8,128)S(1)}, u32[]{:S(2)}, u32[]{:S(2)}) collective-permute-start(f32[2,16,256]{2,1,0:T(8,128)} %get-tuple-element.22), channel_id=1, source_target_pairs={{0,64},{16,80},{32,96},{48,112},{64,0},{80,16},{96,32},{112,48},{1... | collective-permute-start | bytes 98312 | tf_op jit(solution)/shard_map/ppermute | solution.py:27
  36.9 2.4 %collective-permute-start.4 = (f32[2,16,256]{2,1,0:T(8,128)}, f32[2,16,256]{2,1,0:T(8,128)S(1)}, u32[]{:S(2)}, u32[]{:S(2)}) collective-permute-start(f32[2,16,256]{2,1,0:T(8,128)} %get-tuple-element.21), channel_id=1, source_target_pairs={{0,80},{16,64},{32,112},{48,96},{64,16},{80,0},{96,48},{112,32},{1... | collective-permute-start | bytes 98312 | tf_op jit(solution)/shard_map/ppermute | solution.py:27
  39.3 0.9 pad_maximum_fusion.1
  40.3 1.6 %collective-permute-start.5 = (f32[2,16,256]{2,1,0:T(8,128)}, f32[2,16,256]{2,1,0:T(8,128)S(1)}, u32[]{:S(2)}, u32[]{:S(2)}) collective-permute-start(f32[2,16,256]{2,1,0:T(8,128)} %get-tuple-element.20), channel_id=1, source_target_pairs={{0,96},{16,112},{32,64},{48,80},{64,32},{80,48},{96,0},{112,16},{1... | collective-permute-start | bytes 98312 | tf_op jit(solution)/shard_map/ppermute | solution.py:27
  41.8 0.8 constant_dynamic-update-slice_fusion.14
  42.6 2.5 %collective-permute-start.6 = (f32[2,16,256]{2,1,0:T(8,128)}, f32[2,16,256]{2,1,0:T(8,128)S(1)}, u32[]{:S(2)}, u32[]{:S(2)}) collective-permute-start(f32[2,16,256]{2,1,0:T(8,128)} %get-tuple-element.19), channel_id=1, source_target_pairs={{0,112},{16,96},{32,80},{48,64},{64,48},{80,32},{96,16},{112,0},{1... | collective-permute-start | bytes 98312 | tf_op jit(solution)/shard_map/ppermute | solution.py:27
  45.1 0.8 constant_dynamic-update-slice_fusion.13
  45.9 3.0 %collective-permute-start.7 = (f32[2,16,256]{2,1,0:T(8,128)}, f32[2,16,256]{2,1,0:T(8,128)S(1)}, u32[]{:S(2)}, u32[]{:S(2)}) collective-permute-start(f32[2,16,256]{2,1,0:T(8,128)} %get-tuple-element.18), channel_id=1, source_target_pairs={{0,128},{16,144},{32,160},{48,176},{64,192},{80,208},{96,224},{112... | collective-permute-start | bytes 98312 | tf_op jit(solution)/shard_map/ppermute | solution.py:27
  48.9 0.8 constant_dynamic-update-slice_fusion.12
  49.6 3.0 %collective-permute-start.8 = (f32[2,16,256]{2,1,0:T(8,128)}, f32[2,16,256]{2,1,0:T(8,128)S(1)}, u32[]{:S(2)}, u32[]{:S(2)}) collective-permute-start(f32[2,16,256]{2,1,0:T(8,128)} %get-tuple-element.17), channel_id=1, source_target_pairs={{0,144},{16,128},{32,176},{48,160},{64,208},{80,192},{96,240},{112... | collective-permute-start | bytes 98312 | tf_op jit(solution)/shard_map/ppermute | solution.py:27
  52.6 4.5 %collective-permute-start.10 = (f32[2,16,256]{2,1,0:T(8,128)}, f32[2,16,256]{2,1,0:T(8,128)S(1)}, u32[]{:S(2)}, u32[]{:S(2)}) collective-permute-start(f32[2,16,256]{2,1,0:T(8,128)} %get-tuple-element.15), channel_id=1, source_target_pairs={{0,176},{16,160},{32,144},{48,128},{64,240},{80,224},{96,208},{112... | collective-permute-start | bytes 98312 | tf_op jit(solution)/shard_map/ppermute | solution.py:27
  57.1 1.3 %collective-permute-start.11 = (f32[2,16,256]{2,1,0:T(8,128)S(1)}, f32[2,16,256]{2,1,0:T(8,128)S(1)}, u32[]{:S(2)}, u32[]{:S(2)}) collective-permute-start(f32[2,16,256]{2,1,0:T(8,128)S(1)} %copy-done.12), channel_id=1, source_target_pairs={{0,192},{16,208},{32,224},{48,240},{64,128},{80,144},{96,160},{112... | collective-permute-start | bytes 98312 | tf_op jit(solution)/shard_map/ppermute | solution.py:27
  58.5 3.1 %collective-permute-start.12 = (f32[2,16,256]{2,1,0:T(8,128)S(1)}, f32[2,16,256]{2,1,0:T(8,128)S(1)}, u32[]{:S(2)}, u32[]{:S(2)}) collective-permute-start(f32[2,16,256]{2,1,0:T(8,128)S(1)} %copy-done.11), channel_id=1, source_target_pairs={{0,208},{16,192},{32,240},{48,224},{64,144},{80,128},{96,176},{112... | collective-permute-start | bytes 98312 | tf_op jit(solution)/shard_map/ppermute | solution.py:27
  61.6 0.9 collective-permute-start.13
  62.5 2.0 %collective-permute-start.14 = (f32[2,16,256]{2,1,0:T(8,128)S(1)}, f32[2,16,256]{2,1,0:T(8,128)S(1)}, u32[]{:S(2)}, u32[]{:S(2)}) collective-permute-start(f32[2,16,256]{2,1,0:T(8,128)S(1)} %copy-done.9), channel_id=1, source_target_pairs={{0,240},{16,224},{32,208},{48,192},{64,176},{80,160},{96,144},{112... | collective-permute-start | bytes 98312 | tf_op jit(solution)/shard_map/ppermute | solution.py:27
  64.6 2.1 %collective-permute-done.13 = f32[2,16,256]{2,1,0:T(8,128)S(1)} collective-permute-done((f32[2,16,256]{2,1,0:T(8,128)S(1)}, f32[2,16,256]{2,1,0:T(8,128)S(1)}, u32[]{:S(2)}, u32[]{:S(2)}) %collective-permute-start.13) | collective-permute-done | bytes 32800 | tf_op jit(solution)/shard_map/ppermute | solution.py:27
  66.7 0.4 collective-permute-done.14
  67.1 0.6 gather_fusion
  67.8 0.6 copy-done.5
  68.5 0.6 copy.29
  69.1 24.7 %scatter_custom_fusion = f32[16,8192]{0,1:T(8,128)} fusion(s32[4096]{0:T(1024)} %bitcast.133, f32[4096,16]{1,0:T(8,128)S(1)} %copy.29, f32[]{:T(128)} %constant.27.clone.1), kind=kCustom, calls=%fused_computation.3 | custom fusion | flops 65536 | bytes 524800 | tf_op jit(solution)/shard_map/scatter-add | solution.py:74
  93.7 2.9 %copy.30 = f32[16,32,256]{2,1,0:T(8,128)S(1)} copy(f32[16,32,256]{0,2,1:T(8,128)} %bitcast.114) | data formatting | bytes 1048576 | tf_op jit(solution)/shard_map/reshape | solution.py:75
  96.8 3.5 %collective-permute-start.15 = (f32[16,32,8]{2,1,0:T(8,128)S(1)}, f32[16,32,8]{2,1,0:T(8,128)S(1)}, u32[]{:S(2)}, u32[]{:S(2)}) collective-permute-start(f32[16,32,8]{2,1,0:T(8,128)S(1)} %get-tuple-element.7), channel_id=1, source_target_pairs={{0,16},{16,32},{32,48},{48,64},{64,80},{80,96},{96,112},{112,128},... | collective-permute-start | bytes 49160 | tf_op jit(solution)/shard_map/ppermute | solution.py:38
  100.6 3.0 %collective-permute-done.15 = f32[16,32,8]{2,1,0:T(8,128)S(1)} collective-permute-done((f32[16,32,8]{2,1,0:T(8,128)S(1)}, f32[16,32,8]{2,1,0:T(8,128)S(1)}, u32[]{:S(2)}, u32[]{:S(2)}) %collective-permute-start.15) | collective-permute-done | bytes 16416 | tf_op jit(solution)/shard_map/ppermute | solution.py:38
  103.6 2.5 %collective-permute-done.16 = f32[16,32,8]{2,1,0:T(8,128)S(1)} collective-permute-done((f32[16,32,8]{2,1,0:T(8,128)S(1)}, f32[16,32,8]{2,1,0:T(8,128)S(1)}, u32[]{:S(2)}, u32[]{:S(2)}) %collective-permute-start.16) | collective-permute-done | bytes 16416 | tf_op jit(solution)/shard_map/ppermute | solution.py:41
  106.1 0.2 pad_maximum_fusion.4
  106.4 4.8 %collective-permute-start.18 = (f32[16,8,272]{2,1,0:T(8,128)S(1)}, f32[16,8,272]{2,1,0:T(8,128)S(1)}, u32[]{:S(2)}, u32[]{:S(2)}) collective-permute-start(f32[16,8,272]{2,1,0:T(8,128)S(1)} %get-tuple-element.6), channel_id=1, source_target_pairs={{1,0},{2,1},{3,2},{4,3},{5,4},{6,5},{7,6},{8,7},{9,8},{10,9},{11,1... | collective-permute-start | bytes 417800 | tf_op jit(solution)/shard_map/ppermute | solution.py:41
  112.3 3.5 %collective-permute-done.17 = f32[16,8,272]{2,1,0:T(8,128)S(1)} collective-permute-done((f32[16,8,272]{2,1,0:T(8,128)S(1)}, f32[16,8,272]{2,1,0:T(8,128)S(1)}, u32[]{:S(2)}, u32[]{:S(2)}) %collective-permute-start.17) | collective-permute-done | bytes 139296 | tf_op jit(solution)/shard_map/ppermute | solution.py:38
  115.8 0.3 pad_maximum_fusion
  116.1 0.4 fusion.9
  116.5 0.2 fusion.8
  116.7 1.4 %slice_subtract_fusion.10 = f32[16,46,270]{2,1,0:T(8,128)S(1)} fusion(f32[16,47,272]{2,1,0:T(8,128)S(1)} %fusion.8, f32[16,48,271]{2,1,0:T(8,128)S(1)} %fusion.9, f32[16,48,272]{2,1,0:T(8,128)S(1)} %pad_maximum_fusion), kind=kLoop, calls=%fused_computation.25 | loop fusion | flops 794880 | bytes 4769280 | tf_op jit(solution)/shard_map/sub | solution.py:50
  118.1 0.4 fusion.7
  118.5 0.2 fusion.6
  118.7 1.4 %slice_subtract_fusion.6 = f32[16,44,268]{2,1,0:T(8,128)S(1)} fusion(f32[16,45,270]{2,1,0:T(8,128)S(1)} %fusion.6, f32[16,46,269]{2,1,0:T(8,128)S(1)} %fusion.7, f32[16,46,270]{2,1,0:T(8,128)S(1)} %slice_subtract_fusion.10), kind=kLoop, calls=%fused_computation.17 | loop fusion | flops 754688 | bytes 4528128 | tf_op jit(solution)/shard_map/sub | solution.py:50
  120.1 0.4 fusion.5
  120.5 0.2 fusion.4
  120.7 1.4 %slice_subtract_fusion.2 = f32[16,42,266]{2,1,0:T(8,128)S(1)} fusion(f32[16,43,268]{2,1,0:T(8,128)S(1)} %fusion.4, f32[16,44,267]{2,1,0:T(8,128)S(1)} %fusion.5, f32[16,44,268]{2,1,0:T(8,128)S(1)} %slice_subtract_fusion.6), kind=kLoop, calls=%fused_computation.9 | loop fusion | flops 715008 | bytes 4290048 | tf_op jit(solution)/shard_map/sub | solution.py:50
  122.1 0.4 fusion.3
  122.5 0.2 fusion.2
  122.7 1.2 slice_subtract_fusion.28
  123.9 0.3 fusion.17
  124.3 1.2 slice_subtract_fusion.24
  125.6 0.3 fusion.15
  126.0 1.2 slice_subtract_fusion.20
  127.2 0.3 fusion.13
  127.7 1.2 slice_subtract_fusion.16
  128.9 0.3 fusion.11
  129.4 1.5 %slice_subtract_fusion.30 = f32[16,32,256]{2,1,0:T(8,128)} fusion(f32[16,33,258]{2,1,0:T(8,128)S(1)} %fusion.10, f32[16,34,257]{2,1,0:T(8,128)S(1)} %fusion.11, f32[16,34,258]{2,1,0:T(8,128)S(1)} %slice_subtract_fusion.16), kind=kLoop, calls=%fused_computation.66 | loop fusion | flops 524288 | bytes 3145728 | tf_op jit(solution)/shard_map/sub | solution.py:50
  (102 shorter events, 3.2 us)
Async XLA Ops:
  0.0 9.5 %copy-start = (s32[1,16]{1,0:T(1,128)S(1)}, s32[1,16]{1,0:T(1,128)}, u32[]{:S(2)}) copy-start(s32[1,16]{1,0:T(1,128)} %param.13) | copy-start | bytes 196
  0.0 1.9 %copy-start.4 = (f32[16,1,4096]{2,1,0:T(1,128)S(1)}, f32[16,1,4096]{2,1,0:T(1,128)}, u32[]{:S(2)}) copy-start(f32[16,1,4096]{2,1,0:T(1,128)} %param.15) | copy-start | bytes 786436
  1.9 6.9 %copy-start.8 = (s32[32,256]{1,0:T(8,128)S(1)}, s32[32,256]{1,0:T(8,128)}, u32[]{:S(2)}) copy-start(s32[32,256]{1,0:T(8,128)} %param.11) | copy-start | bytes 98308
  2.6 6.2 %copy-start.2 = (f32[32,256]{1,0:T(8,128)S(1)}, f32[32,256]{1,0:T(8,128)}, u32[]{:S(2)}) copy-start(f32[32,256]{1,0:T(8,128)} %param.10) | copy-start | bytes 98308
  2.6 6.2 %copy-start.3 = (f32[32,256]{1,0:T(8,128)S(1)}, f32[32,256]{1,0:T(8,128)}, u32[]{:S(2)}) copy-start(f32[32,256]{1,0:T(8,128)} %param.9) | copy-start | bytes 98308
  2.7 6.8 %copy-start.6 = (s32[1,4096]{1,0:T(1,128)S(1)}, s32[1,4096]{1,0:T(1,128)}, u32[]{:S(2)}) copy-start(s32[1,4096]{1,0:T(1,128)} %param.12) | copy-start | bytes 49156
  2.8 14.8 %copy-start.1 = (f32[16,32,256]{2,1,0:T(8,128)S(1)}, f32[16,32,256]{2,1,0:T(8,128)}, u32[]{:S(2)}) copy-start(f32[16,32,256]{2,1,0:T(8,128)} %param.8) | copy-start | bytes 1572868
  3.8 36.5 %collective-permute-start = (f32[2,16,256]{2,1,0:T(8,128)}, f32[2,16,256]{2,1,0:T(8,128)}, u32[]{:S(2)}, u32[]{:S(2)}) collective-permute-start(f32[2,16,256]{2,1,0:T(8,128)} %get-tuple-element.25), channel_id=1, source_target_pairs={{0,16},{16,0},{32,48},{48,32},{64,80},{80,64},{96,112},{112,96},{1... | collective-permute-start | bytes 98312 | tf_op jit(solution)/shard_map/ppermute | solution.py:27
  7.0 35.5 %collective-permute-start.1 = (f32[2,16,256]{2,1,0:T(8,128)}, f32[2,16,256]{2,1,0:T(8,128)}, u32[]{:S(2)}, u32[]{:S(2)}) collective-permute-start(f32[2,16,256]{2,1,0:T(8,128)} %get-tuple-element.24), channel_id=1, source_target_pairs={{0,32},{16,48},{32,0},{48,16},{64,96},{80,112},{96,64},{112,80},{1... | collective-permute-start | bytes 98312 | tf_op jit(solution)/shard_map/ppermute | solution.py:27
  7.1 38.8 %collective-permute-start.2 = (f32[2,16,256]{2,1,0:T(8,128)}, f32[2,16,256]{2,1,0:T(8,128)}, u32[]{:S(2)}, u32[]{:S(2)}) collective-permute-start(f32[2,16,256]{2,1,0:T(8,128)} %get-tuple-element.23), channel_id=1, source_target_pairs={{0,48},{16,32},{32,16},{48,0},{64,112},{80,96},{96,80},{112,64},{1... | collective-permute-start | bytes 98312 | tf_op jit(solution)/shard_map/ppermute | solution.py:27
  8.9 1.8 %collective-permute-start.19 = (f32[3,32,8]{2,1,0:T(8,128)S(1)}, f32[3,32,8]{2,1,0:T(8,128)S(1)}, u32[]{:S(2)}, u32[]{:S(2)}) collective-permute-start(f32[3,32,8]{2,1,0:T(8,128)S(1)} %get-tuple-element.28), channel_id=1, source_target_pairs={{0,16},{16,32},{32,48},{48,64},{64,80},{80,96},{96,112},{112,128},... | collective-permute-start | bytes 9224 | tf_op jit(solution)/shard_map/ppermute | solution.py:38
  9.0 3.5 %collective-permute-start.20 = (f32[3,32,8]{2,1,0:T(8,128)S(1)}, f32[3,32,8]{2,1,0:T(8,128)S(1)}, u32[]{:S(2)}, u32[]{:S(2)}) collective-permute-start(f32[3,32,8]{2,1,0:T(8,128)S(1)} %get-tuple-element.29), channel_id=1, source_target_pairs={{16,0},{32,16},{48,32},{64,48},{80,64},{96,80},{112,96},{128,112},... | collective-permute-start | bytes 9224 | tf_op jit(solution)/shard_map/ppermute | solution.py:41
  9.5 10.7 %copy-start.7 = (s32[4096,1]{0,1:T(1,128)}, s32[4096,1]{0,1:T(1,128)S(1)}, u32[]{:S(2)}) copy-start(s32[4096,1]{0,1:T(1,128)S(1)} %compare_select_fusion) | copy-start | bytes 49156
  12.6 21.2 %collective-permute-start.21 = (f32[3,8,272]{2,1,0:T(8,128)S(1)}, f32[3,8,272]{2,1,0:T(8,128)S(1)}, u32[]{:S(2)}, u32[]{:S(2)}) collective-permute-start(f32[3,8,272]{2,1,0:T(8,128)S(1)} %get-tuple-element.26), channel_id=1, source_target_pairs={{0,1},{1,2},{2,3},{3,4},{4,5},{5,6},{6,7},{7,8},{8,9},{9,10},{10,1... | collective-permute-start | bytes 78344 | tf_op jit(solution)/shard_map/ppermute | solution.py:38
  13.8 23.0 %collective-permute-start.22 = (f32[3,8,272]{2,1,0:T(8,128)S(1)}, f32[3,8,272]{2,1,0:T(8,128)}, u32[]{:S(2)}, u32[]{:S(2)}) collective-permute-start(f32[3,8,272]{2,1,0:T(8,128)S(1)} %get-tuple-element.27), channel_id=1, source_target_pairs={{1,0},{2,1},{3,2},{4,3},{5,4},{6,5},{7,6},{8,7},{9,8},{10,9},{11,1... | collective-permute-start | bytes 78344 | tf_op jit(solution)/shard_map/ppermute | solution.py:41
  33.7 23.4 %copy-start.12 = (f32[2,16,256]{2,1,0:T(8,128)S(1)}, f32[2,16,256]{2,1,0:T(8,128)}, u32[]{:S(2)}) copy-start(f32[2,16,256]{2,1,0:T(8,128)} %get-tuple-element.14) | copy-start | bytes 98308
  33.7 24.7 %copy-start.11 = (f32[2,16,256]{2,1,0:T(8,128)S(1)}, f32[2,16,256]{2,1,0:T(8,128)}, u32[]{:S(2)}) copy-start(f32[2,16,256]{2,1,0:T(8,128)} %get-tuple-element.13) | copy-start | bytes 98308
  33.7 27.9 %copy-start.10 = (f32[2,16,256]{2,1,0:T(8,128)S(1)}, f32[2,16,256]{2,1,0:T(8,128)}, u32[]{:S(2)}) copy-start(f32[2,16,256]{2,1,0:T(8,128)} %get-tuple-element.12) | copy-start | bytes 98308
  33.7 28.7 %copy-start.9 = (f32[2,16,256]{2,1,0:T(8,128)S(1)}, f32[2,16,256]{2,1,0:T(8,128)}, u32[]{:S(2)}) copy-start(f32[2,16,256]{2,1,0:T(8,128)} %get-tuple-element.11) | copy-start | bytes 98308
  33.8 15.9 %collective-permute-start.3 = (f32[2,16,256]{2,1,0:T(8,128)}, f32[2,16,256]{2,1,0:T(8,128)S(1)}, u32[]{:S(2)}, u32[]{:S(2)}) collective-permute-start(f32[2,16,256]{2,1,0:T(8,128)} %get-tuple-element.22), channel_id=1, source_target_pairs={{0,64},{16,80},{32,96},{48,112},{64,0},{80,16},{96,32},{112,48},{1... | collective-permute-start | bytes 98312 | tf_op jit(solution)/shard_map/ppermute | solution.py:27
  36.9 15.7 %collective-permute-start.4 = (f32[2,16,256]{2,1,0:T(8,128)}, f32[2,16,256]{2,1,0:T(8,128)S(1)}, u32[]{:S(2)}, u32[]{:S(2)}) collective-permute-start(f32[2,16,256]{2,1,0:T(8,128)} %get-tuple-element.21), channel_id=1, source_target_pairs={{0,80},{16,64},{32,112},{48,96},{64,16},{80,0},{96,48},{112,32},{1... | collective-permute-start | bytes 98312 | tf_op jit(solution)/shard_map/ppermute | solution.py:27
  40.3 12.3 %collective-permute-start.5 = (f32[2,16,256]{2,1,0:T(8,128)}, f32[2,16,256]{2,1,0:T(8,128)S(1)}, u32[]{:S(2)}, u32[]{:S(2)}) collective-permute-start(f32[2,16,256]{2,1,0:T(8,128)} %get-tuple-element.20), channel_id=1, source_target_pairs={{0,96},{16,112},{32,64},{48,80},{64,32},{80,48},{96,0},{112,16},{1... | collective-permute-start | bytes 98312 | tf_op jit(solution)/shard_map/ppermute | solution.py:27
  42.6 14.5 %collective-permute-start.6 = (f32[2,16,256]{2,1,0:T(8,128)}, f32[2,16,256]{2,1,0:T(8,128)S(1)}, u32[]{:S(2)}, u32[]{:S(2)}) collective-permute-start(f32[2,16,256]{2,1,0:T(8,128)} %get-tuple-element.19), channel_id=1, source_target_pairs={{0,112},{16,96},{32,80},{48,64},{64,48},{80,32},{96,16},{112,0},{1... | collective-permute-start | bytes 98312 | tf_op jit(solution)/shard_map/ppermute | solution.py:27
  45.9 12.6 %collective-permute-start.7 = (f32[2,16,256]{2,1,0:T(8,128)}, f32[2,16,256]{2,1,0:T(8,128)S(1)}, u32[]{:S(2)}, u32[]{:S(2)}) collective-permute-start(f32[2,16,256]{2,1,0:T(8,128)} %get-tuple-element.18), channel_id=1, source_target_pairs={{0,128},{16,144},{32,160},{48,176},{64,192},{80,208},{96,224},{112... | collective-permute-start | bytes 98312 | tf_op jit(solution)/shard_map/ppermute | solution.py:27
  49.6 12.0 %collective-permute-start.8 = (f32[2,16,256]{2,1,0:T(8,128)}, f32[2,16,256]{2,1,0:T(8,128)S(1)}, u32[]{:S(2)}, u32[]{:S(2)}) collective-permute-start(f32[2,16,256]{2,1,0:T(8,128)} %get-tuple-element.17), channel_id=1, source_target_pairs={{0,144},{16,128},{32,176},{48,160},{64,208},{80,192},{96,240},{112... | collective-permute-start | bytes 98312 | tf_op jit(solution)/shard_map/ppermute | solution.py:27
  52.6 9.9 %collective-permute-start.9 = (f32[2,16,256]{2,1,0:T(8,128)}, f32[2,16,256]{2,1,0:T(8,128)S(1)}, u32[]{:S(2)}, u32[]{:S(2)}) collective-permute-start(f32[2,16,256]{2,1,0:T(8,128)} %get-tuple-element.16), channel_id=1, source_target_pairs={{0,160},{16,176},{32,128},{48,144},{64,224},{80,240},{96,192},{112... | collective-permute-start | bytes 98312 | tf_op jit(solution)/shard_map/ppermute | solution.py:27
  52.6 11.9 %collective-permute-start.10 = (f32[2,16,256]{2,1,0:T(8,128)}, f32[2,16,256]{2,1,0:T(8,128)S(1)}, u32[]{:S(2)}, u32[]{:S(2)}) collective-permute-start(f32[2,16,256]{2,1,0:T(8,128)} %get-tuple-element.15), channel_id=1, source_target_pairs={{0,176},{16,160},{32,144},{48,128},{64,240},{80,224},{96,208},{112... | collective-permute-start | bytes 98312 | tf_op jit(solution)/shard_map/ppermute | solution.py:27
  57.1 7.4 %collective-permute-start.11 = (f32[2,16,256]{2,1,0:T(8,128)S(1)}, f32[2,16,256]{2,1,0:T(8,128)S(1)}, u32[]{:S(2)}, u32[]{:S(2)}) collective-permute-start(f32[2,16,256]{2,1,0:T(8,128)S(1)} %copy-done.12), channel_id=1, source_target_pairs={{0,192},{16,208},{32,224},{48,240},{64,128},{80,144},{96,160},{112... | collective-permute-start | bytes 98312 | tf_op jit(solution)/shard_map/ppermute | solution.py:27
  58.5 6.2 %collective-permute-start.12 = (f32[2,16,256]{2,1,0:T(8,128)S(1)}, f32[2,16,256]{2,1,0:T(8,128)S(1)}, u32[]{:S(2)}, u32[]{:S(2)}) collective-permute-start(f32[2,16,256]{2,1,0:T(8,128)S(1)} %copy-done.11), channel_id=1, source_target_pairs={{0,208},{16,192},{32,240},{48,224},{64,144},{80,128},{96,176},{112... | collective-permute-start | bytes 98312 | tf_op jit(solution)/shard_map/ppermute | solution.py:27
  61.6 5.1 %collective-permute-start.13 = (f32[2,16,256]{2,1,0:T(8,128)S(1)}, f32[2,16,256]{2,1,0:T(8,128)S(1)}, u32[]{:S(2)}, u32[]{:S(2)}) collective-permute-start(f32[2,16,256]{2,1,0:T(8,128)S(1)} %copy-done.10), channel_id=1, source_target_pairs={{0,224},{16,240},{32,192},{48,208},{64,160},{80,176},{96,128},{112... | collective-permute-start | bytes 98312 | tf_op jit(solution)/shard_map/ppermute | solution.py:27
  62.5 4.6 %collective-permute-start.14 = (f32[2,16,256]{2,1,0:T(8,128)S(1)}, f32[2,16,256]{2,1,0:T(8,128)S(1)}, u32[]{:S(2)}, u32[]{:S(2)}) collective-permute-start(f32[2,16,256]{2,1,0:T(8,128)S(1)} %copy-done.9), channel_id=1, source_target_pairs={{0,240},{16,224},{32,208},{48,192},{64,176},{80,160},{96,144},{112... | collective-permute-start | bytes 98312 | tf_op jit(solution)/shard_map/ppermute | solution.py:27
  67.7 0.7 copy-start.5
  96.8 6.8 %collective-permute-start.15 = (f32[16,32,8]{2,1,0:T(8,128)S(1)}, f32[16,32,8]{2,1,0:T(8,128)S(1)}, u32[]{:S(2)}, u32[]{:S(2)}) collective-permute-start(f32[16,32,8]{2,1,0:T(8,128)S(1)} %get-tuple-element.7), channel_id=1, source_target_pairs={{0,16},{16,32},{32,48},{48,64},{64,80},{80,96},{96,112},{112,128},... | collective-permute-start | bytes 49160 | tf_op jit(solution)/shard_map/ppermute | solution.py:38
  100.3 5.8 %collective-permute-start.16 = (f32[16,32,8]{2,1,0:T(8,128)S(1)}, f32[16,32,8]{2,1,0:T(8,128)S(1)}, u32[]{:S(2)}, u32[]{:S(2)}) collective-permute-start(f32[16,32,8]{2,1,0:T(8,128)S(1)} %get-tuple-element.8), channel_id=1, source_target_pairs={{16,0},{32,16},{48,32},{64,48},{80,64},{96,80},{112,96},{128,112},... | collective-permute-start | bytes 49160 | tf_op jit(solution)/shard_map/ppermute | solution.py:41
  106.3 9.5 %collective-permute-start.17 = (f32[16,8,272]{2,1,0:T(8,128)S(1)}, f32[16,8,272]{2,1,0:T(8,128)S(1)}, u32[]{:S(2)}, u32[]{:S(2)}) collective-permute-start(f32[16,8,272]{2,1,0:T(8,128)S(1)} %get-tuple-element.5), channel_id=1, source_target_pairs={{0,1},{1,2},{2,3},{3,4},{4,5},{5,6},{6,7},{7,8},{8,9},{9,10},{10,1... | collective-permute-start | bytes 417800 | tf_op jit(solution)/shard_map/ppermute | solution.py:38
  106.4 9.4 %collective-permute-start.18 = (f32[16,8,272]{2,1,0:T(8,128)S(1)}, f32[16,8,272]{2,1,0:T(8,128)S(1)}, u32[]{:S(2)}, u32[]{:S(2)}) collective-permute-start(f32[16,8,272]{2,1,0:T(8,128)S(1)} %get-tuple-element.6), channel_id=1, source_target_pairs={{1,0},{2,1},{3,2},{4,3},{5,4},{6,5},{7,6},{8,7},{9,8},{10,9},{11,1... | collective-permute-start | bytes 417800 | tf_op jit(solution)/shard_map/ppermute | solution.py:41
